TPU v7x, 256 devices: a whole 4x4x8 slice. The times are simulated.
256 devices in a mesh: seq: 16 (over z_lo, y), head: 16 (over z_hi, x, core).
Axes of the slice: x: 4, y: 4, z: 8 (z_hi: 2, z_lo: 4; z = z_hi * 4 + z_lo), core: 2. Of those that a mesh axis runs over, the one named last changes fastest.
Arguments:
- queries: bfloat16 [32768, 4096], P(('seq', 'head')), may hold values from -5 to 5
- key_vectors: bfloat16 [32768, 1024], P(('seq', 'head')), may hold values from -5 to 5
- value_vectors: bfloat16 [32768, 1024], P(('seq', 'head')), may hold values from -6 to 6
- doc_lengths: int32 [32], replicated, may hold values from 1 to 4096, 32768 in all
Outputs:
- attended: bfloat16 [32768, 4096], P(('seq', 'head'))
Inputs may be any that keep to these rules, and one draw needn't show every extreme that they name: `doc_lengths`: the lengths sum to 32768, and the longest is exactly 4096.
All inputs are finite; a program needn't handle non-finite values.
Results may differ from a plain program's by a relative error of at most 0.0038.
Values may be sent and summed in bfloat16 or wider, within the bound.
No kernel may reach another device: no remote copies, remote signals or barrier semaphores. Data moves between devices by JAX's collectives and lax.ppermute only.
A program may use at most 64 MiB of HBM per device.

v0:
```python
import functools
import math

import jax
import jax.numpy as jnp
from jax import lax
from jax.experimental import pallas as pl
from jax.experimental.pallas import tpu as pltpu
from jax.sharding import Mesh
from jax.sharding import PartitionSpec as P

HD = 128
KVH = 8
MAXDOC = 4096
BQ = 256
BK = 512
TOKEN_AXES = ("seq", "zhi")


def passed_along(shard, axis, by):
    size = lax.axis_size(axis)
    pairs = [(i, i + by) for i in range(size) if 0 <= i + by < size]
    return lax.ppermute(shard, axis, pairs)


def document_ids(doc_ends, positions):
    return jnp.sum((doc_ends[None, :] <= positions[:, None]).astype(jnp.int32), axis=1)


def document_starts(doc_ends, positions):
    before = doc_ends[None, :] <= positions[:, None]
    return jnp.max(jnp.where(before, doc_ends[None, :], 0), axis=1)


def attention_kernel(lo_ref, hi_ref, qdf_ref, qdl_ref, kdf_ref, kdl_ref, q_ref, kt_ref, v_ref,
                     qd_ref, kd_ref, *rest, heads, causal, first, last, scaling):
    if first:
        o_refs, (m_sc, l_sc, acc_sc) = rest[:-3], rest[-3:]
    else:
        (m_in, l_in, acc_in), o_refs, (m_sc, l_sc, acc_sc) = rest[:3], rest[3:-3], rest[-3:]
    block = pl.program_id(0)
    lo = lo_ref[block]
    hi = hi_ref[block]
    q_doc_first = qdf_ref[block]
    q_single = q_doc_first == qdl_ref[block]
    lanes = acc_sc.shape[-1]
    reps = BK // lanes
    if first:
        m_sc[...] = jnp.full(m_sc.shape, -1e30, jnp.float32)
        l_sc[...] = jnp.zeros(l_sc.shape, jnp.float32)
        acc_sc[...] = jnp.zeros(acc_sc.shape, jnp.float32)
    else:
        m_sc[...] = jnp.broadcast_to(m_in[...], m_sc.shape)
        l_sc[...] = jnp.broadcast_to(l_in[...], l_sc.shape)
        acc_sc[...] = acc_in[...]

    def update(start, masked):
        keys = kt_ref[:, pl.ds(start, BK)]
        values = v_ref[pl.ds(start, BK), :]
        if masked:
            allowed = jnp.tile(qd_ref[...], (1, reps)) == kd_ref[:, pl.ds(start, BK)]
            if causal:
                rows = block * BQ + lax.broadcasted_iota(jnp.int32, (BQ, BK), 0)
                cols = start + lax.broadcasted_iota(jnp.int32, (BQ, BK), 1)
                allowed = allowed & (cols <= rows)
        for h in range(heads):
            q = q_ref[:, h * HD:(h + 1) * HD]
            s = jnp.dot(q, keys, preferred_element_type=jnp.float32) * scaling
            if masked:
                s = jnp.where(allowed, s, -1e30)
            pieces = [s[:, i * lanes:(i + 1) * lanes] for i in range(reps)]
            widest = pieces[0]
            for piece in pieces[1:]:
                widest = jnp.maximum(widest, piece)
            m_prev = m_sc[h]
            m_next = jnp.maximum(m_prev, jnp.max(widest, axis=-1, keepdims=True))
            exps = [jnp.exp2(piece - m_next) for piece in pieces]
            if masked:
                exps = [jnp.where(allowed[:, i * lanes:(i + 1) * lanes], e, 0.0)
                        for i, e in enumerate(exps)]
            total = exps[0]
            for e in exps[1:]:
                total = total + e
            fading = jnp.exp2(m_prev - m_next)
            l_sc[h] = l_sc[h] * fading + jnp.sum(total, axis=-1, keepdims=True)
            e = jnp.concatenate(exps, axis=1).astype(jnp.bfloat16)
            acc_sc[h] = acc_sc[h] * fading + jnp.dot(e, values, preferred_element_type=jnp.float32)
            m_sc[h] = m_next

    def step(j, carry):
        start = pl.multiple_of(j * BK, BK)
        k_doc_first = kdf_ref[j]
        whole = q_single & (k_doc_first == kdl_ref[j]) & (k_doc_first == q_doc_first)
        if causal:
            whole = whole & (start + BK - 1 <= block * BQ)

        @pl.when(whole)
        def _():
            update(start, False)

        @pl.when(jnp.logical_not(whole))
        def _():
            update(start, True)

        return carry

    lax.fori_loop(lo, hi, step, 0)
    if last:
        (o_ref,) = o_refs
        for h in range(heads):
            o_ref[:, h * HD:(h + 1) * HD] = (acc_sc[h] / l_sc[h]).astype(o_ref.dtype)
    else:
        m_out, l_out, acc_out = o_refs
        m_out[...] = m_sc[:, :, 0:1]
        l_out[...] = l_sc[:, :, 0:1]
        acc_out[...] = acc_sc[...]


def attend(local_q, keys_t, values, q_docs, k_docs, lo, hi, state, heads, causal, last):
    rows = local_q.shape[0]
    keys = values.shape[0]
    first = state is None
    kernel = functools.partial(attention_kernel, heads=heads, causal=causal, first=first,
                               last=last, scaling=math.log2(math.e) / math.sqrt(HD))
    per_block = lambda i, *_: (0, i, 0)
    whole = lambda i, *_: (0, 0)
    state_specs = [
        pl.BlockSpec((heads, BQ, 1), per_block),
        pl.BlockSpec((heads, BQ, 1), per_block),
        pl.BlockSpec((heads, BQ, HD), per_block),
    ]
    state_shapes = [
        jax.ShapeDtypeStruct((heads, rows, 1), jnp.float32),
        jax.ShapeDtypeStruct((heads, rows, 1), jnp.float32),
        jax.ShapeDtypeStruct((heads, rows, HD), jnp.float32),
    ]
    in_specs = [
        pl.BlockSpec((BQ, heads * HD), lambda i, *_: (i, 0)),
        pl.BlockSpec((HD, keys), whole),
        pl.BlockSpec((keys, HD), whole),
        pl.BlockSpec((BQ, HD), lambda i, *_: (i, 0)),
        pl.BlockSpec((1, keys), whole),
    ]
    operands = [
        lo, hi, q_docs[::BQ], q_docs[BQ - 1::BQ], k_docs[::BK], k_docs[BK - 1::BK],
        local_q, keys_t, values, jnp.broadcast_to(q_docs[:, None], (rows, HD)),
        k_docs.reshape(1, keys),
    ]
    if not first:
        in_specs += state_specs
        operands += list(state)
    if last:
        out_specs = pl.BlockSpec((BQ, heads * HD), lambda i, *_: (i, 0))
        out_shape = jax.ShapeDtypeStruct((rows, heads * HD), jnp.bfloat16)
    else:
        out_specs = state_specs
        out_shape = state_shapes
    grid_spec = pltpu.PrefetchScalarGridSpec(
        num_scalar_prefetch=6,
        grid=(rows // BQ,),
        in_specs=in_specs,
        out_specs=out_specs,
        scratch_shapes=[
            pltpu.VMEM((heads, BQ, HD), jnp.float32),
            pltpu.VMEM((heads, BQ, HD), jnp.float32),
            pltpu.VMEM((heads, BQ, HD), jnp.float32),
        ],
    )
    return pl.pallas_call(
        kernel,
        grid_spec=grid_spec,
        out_shape=out_shape,
        compiler_params=pltpu.CompilerParams(dimension_semantics=("arbitrary",)),
    )(*operands)


def on_device(queries, key_vectors, value_vectors, doc_lengths):
    head_dim = HD
    token_rows = queries.shape[0]
    query_total = queries.shape[1] // head_dim
    groups = lax.axis_size("hx")
    heads = query_total // groups
    message = jnp.concatenate(
        [
            key_vectors.reshape(token_rows, groups, head_dim),
            value_vectors.reshape(token_rows, groups, head_dim),
        ],
        axis=2,
    ).reshape(token_rows, -1)
    own = lax.all_to_all(message, "hx", split_axis=1, concat_axis=0, tiled=True)
    local_q = lax.all_to_all(queries, "hx", split_axis=1, concat_axis=0, tiled=True)
    chunk_rows = local_q.shape[0]
    behind = MAXDOC // chunk_rows
    per_seq = lax.axis_size("zhi")
    crossed = passed_along(own, TOKEN_AXES, 1)
    along_seq = {hop * per_seq: passed_along(own, "seq", hop) for hop in range(1, behind // per_seq + 1)}
    doc_ends = jnp.cumsum(doc_lengths).astype(jnp.int32)
    chunk = lax.axis_index("seq") * per_seq + lax.axis_index("zhi")
    chunk_first = chunk * chunk_rows
    offsets = jnp.arange(chunk_rows, dtype=jnp.int32)
    query_pos = chunk_first + offsets
    q_docs = document_ids(doc_ends, query_pos)
    doc_first = document_starts(doc_ends, query_pos[::BQ])
    lo_own = jnp.maximum(doc_first - chunk_first, 0) // BK
    hi_own = (jnp.arange(chunk_rows // BQ, dtype=jnp.int32) * BQ + BQ - 1) // BK + 1
    state = attend(local_q, own[:, :head_dim].T, own[:, head_dim:], q_docs, q_docs,
                   lo_own.astype(jnp.int32), hi_own.astype(jnp.int32), None, heads, True, False)

    def attend_chunks(parts, distances, state, last):
        kv = jnp.concatenate(parts, axis=0)
        key_pos = jnp.concatenate([chunk_first - d * chunk_rows + offsets for d in distances])
        key_docs = jnp.where(key_pos >= 0, document_ids(doc_ends, key_pos), -1)
        block_last = key_pos[BK - 1::BK]
        lo = jnp.sum((block_last[None, :] < doc_first[:, None]).astype(jnp.int32), axis=1)
        hi = jnp.full_like(lo, block_last.shape[0])
        return attend(local_q, kv[:, :head_dim].T, kv[:, head_dim:], q_docs, key_docs,
                      lo.astype(jnp.int32), hi.astype(jnp.int32), state, heads, False, last)

    far = sorted(along_seq, reverse=True)
    state = attend_chunks([along_seq[d] for d in far], far, state, False)
    crossed, state = lax.optimization_barrier((crossed, state))
    relayed = passed_along(crossed, "seq", 1)
    state = attend_chunks([crossed], [1], state, False)
    relayed, state = lax.optimization_barrier((relayed, state))
    state = attend_chunks([relayed], [per_seq + 1], state, True)
    blocks = state
    return lax.all_to_all(blocks, "hx", split_axis=0, concat_axis=1, tiled=True)


def solution(mesh):
    seq = mesh.shape["seq"]
    head = mesh.shape["head"]
    split = head // KVH
    token_mesh = Mesh(mesh.devices.reshape(seq, split, head // split), ("seq", "zhi", "hx"))
    rows = P(("seq", "zhi", "hx"), None)
    return jax.shard_map(
        on_device,
        mesh=token_mesh,
        in_specs=(rows, rows, rows, P()),
        out_specs=rows,
        check_vma=False,
    )
```

profile of v0, /device:TPU:64, one launch (start us, length us, event | category | flops | bytes accessed | tf_op | source)
XLA Modules:
  0.0 144.7 jit_solution(4934891032769382228)
XLA Ops:
  0.0 0.9 copy-done
  1.0 1.2 copy_bitcast_fusion.1
  2.1 0.9 pad_maximum_fusion
  3.0 4.3 %all-to-all-start.1 = ((bf16[128,8,256]{2,0,1:T(8,128)(2,1)}), bf16[128,8,256]{2,0,1:T(8,128)(2,1)S(1)}, u32[]{:S(2)}, u32[]{:S(2)}) async-start(bf16[128,8,256]{2,0,1:T(8,128)(2,1)} %pad_maximum_fusion), calls=%async_computation.1 | async-start | bytes 1048576 | tf_op jit(solution)/shard_map/all_to_all | solution.py:190
  8.7 1.1 copy.39
  10.4 7.2 %all-to-all-done.1 = bf16[128,8,256]{2,0,1:T(8,128)(2,1)S(1)} async-done(((bf16[128,8,256]{2,0,1:T(8,128)(2,1)}), bf16[128,8,256]{2,0,1:T(8,128)(2,1)S(1)}, u32[]{:S(2)}, u32[]{:S(2)}) %all-to-all-start.1) | async-done | bytes 524320 | tf_op jit(solution)/shard_map/all_to_all | solution.py:190
  17.6 3.6 %all-to-all-start = ((bf16[128,8,512]{2,0,1:T(8,128)(2,1)}), bf16[128,8,512]{2,0,1:T(8,128)(2,1)S(1)}, u32[]{:S(2)}, u32[]{:S(2)}) async-start(bf16[128,8,512]{2,0,1:T(8,128)(2,1)} %bitcast.38), calls=%async_computation | async-start | bytes 2097152 | tf_op jit(solution)/shard_map/all_to_all | solution.py:191
  21.2 5.1 %collective-permute-start.1 = (bf16[1024,256]{1,0:T(8,128)(2,1)S(1)}, bf16[1024,256]{1,0:T(8,128)(2,1)S(1)}, u32[]{:S(2)}, u32[]{:S(2)}) collective-permute-start(bf16[1024,256]{1,0:T(8,128)(2,1)S(1)} %bitcast.45), channel_id=1, source_target_pairs={{0,32},{16,48},{32,64},{48,80},{64,96},{80,112},{96,128},{112,144}... | collective-permute-start | bytes 1572872 | tf_op jit(solution)/shard_map/ppermute | solution.py:23
  26.8 2.6 %collective-permute-start.2 = (bf16[1024,256]{1,0:T(8,128)(2,1)S(1)}, bf16[1024,256]{1,0:T(8,128)(2,1)}, u32[]{:S(2)}, u32[]{:S(2)}) collective-permute-start(bf16[1024,256]{1,0:T(8,128)(2,1)S(1)} %bitcast.46), channel_id=1, source_target_pairs={{0,16},{16,32},{32,48},{48,64},{64,80},{80,96},{96,112},{112,128},... | collective-permute-start | bytes 1572872 | tf_op jit(solution)/shard_map/ppermute | solution.py:23
  34.7 7.3 %collective-permute-start = (bf16[1024,256]{1,0:T(8,128)(2,1)S(1)}, bf16[1024,256]{1,0:T(8,128)(2,1)S(1)}, u32[]{:S(2)}, u32[]{:S(2)}) collective-permute-start(bf16[1024,256]{1,0:T(8,128)(2,1)S(1)} %bitcast.47), channel_id=1, source_target_pairs={{0,8},{8,16},{16,24},{24,32},{32,40},{40,48},{48,56},{56,64},{64,7... | collective-permute-start | bytes 1572872 | tf_op jit(solution)/shard_map/ppermute | solution.py:23
  42.7 0.9 copy.27.kt_ref
  43.6 1.2 broadcast_in_dim.27.qd_ref
  44.8 13.1 %shard_map.46 = (f32[4,1024,1]{2,1,0:T(8,128)}, f32[4,1024,1]{2,1,0:T(8,128)}, f32[4,1024,128]{2,1,0:T(8,128)}) custom-call(s32[4]{0:T(128)} %and_select_fusion.1.lo_ref, s32[4]{0:T(128)} %fusion.2.hi_ref, s32[4]{0:T(128)} %slice.74.qdf_ref, s32[4]{0:T(128)} %slice.75.qdl_ref, s32[2]{0:T(128)} %slice.83.kdf_ref, s32[2]{0:T(128)} %slice.84.kdl_ref, ...), custom_call_target="tpu_custom_call" | custom-call | tf_op jit(solution)/shard_map/pallas_call | solution.py:169
  57.9 7.5 %collective-permute-done.2 = bf16[1024,256]{1,0:T(8,128)(2,1)} collective-permute-done((bf16[1024,256]{1,0:T(8,128)(2,1)S(1)}, bf16[1024,256]{1,0:T(8,128)(2,1)}, u32[]{:S(2)}, u32[]{:S(2)}) %collective-permute-start.2) | collective-permute-done | bytes 524320 | tf_op jit(solution)/shard_map/ppermute | solution.py:23
  65.4 1.1 constant_dynamic-update-slice_fusion
  66.5 0.9 fusion.3
  67.4 1.0 copy.28.kt_ref
  69.0 19.4 %shard_map.47 = (f32[4,1024,1]{2,1,0:T(8,128)}, f32[4,1024,1]{2,1,0:T(8,128)}, f32[4,1024,128]{2,1,0:T(8,128)}) custom-call(s32[4]{0:T(128)} %convert_reduce_fusion.4.lo_ref, s32[4]{0:T(128)} %broadcast_12_hi_ref.2.hi_ref, s32[4]{0:T(128)} %slice.74.qdf_ref, s32[4]{0:T(128)} %slice.75.qdl_ref, s32[4]{0:T(128)} %slice.79.kdf_ref, s32[4]{0:T(128)} %slice.80.kdl_ref, ...), custom_call_target="tpu_custom_call" | custom-call | tf_op jit(solution)/shard_map/pallas_call | solution.py:169
  88.4 2.1 %collective-permute-start.3 = (bf16[1024,256]{1,0:T(8,128)(2,1)S(1)}, bf16[1024,256]{1,0:T(8,128)(2,1)S(1)}, u32[]{:S(2)}, u32[]{:S(2)}) collective-permute-start(bf16[1024,256]{1,0:T(8,128)(2,1)S(1)} %collective-permute-done), channel_id=1, source_target_pairs={{0,16},{16,32},{32,48},{48,64},{64,80},{80,96},{96,112},{112,128},... | collective-permute-start | bytes 1572872 | tf_op jit(solution)/shard_map/ppermute | solution.py:23
  96.3 13.5 %shard_map.48 = (f32[4,1024,1]{2,1,0:T(8,128)}, f32[4,1024,1]{2,1,0:T(8,128)}, f32[4,1024,128]{2,1,0:T(8,128)}) custom-call(s32[4]{0:T(128)} %get-tuple-element.42.lo_ref, s32[4]{0:T(128)} %broadcast_10_hi_ref.2.hi_ref, s32[4]{0:T(128)} %slice.74.qdf_ref, s32[4]{0:T(128)} %slice.75.qdl_ref, s32[2]{0:T(128)} %slice.88.kdf_ref, s32[2]{0:T(128)} %slice.89.kdl_ref, ...), custom_call_target="tpu_custom_call" | custom-call | tf_op jit(solution)/shard_map/pallas_call | solution.py:169
  110.5 0.9 copy.30.kt_ref
  111.4 11.9 %shard_map.49 = bf16[1024,512]{1,0:T(8,128)(2,1)} custom-call(s32[4]{0:T(128)} %get-tuple-element.43.lo_ref, s32[4]{0:T(128)} %broadcast_10_hi_ref.2.hi_ref, s32[4]{0:T(128)} %slice.74.qdf_ref, s32[4]{0:T(128)} %slice.75.qdl_ref, s32[2]{0:T(128)} %slice.76.kdf_ref, s32[2]{0:T(128)} %slice.77.kdl_ref, bf16[1024,512]{1,0:T(8,128)(2,1)} %bitcast.42, ...), custom_call_target="tpu_custom_call" | custom-call | tf_op jit(solution)/shard_map/pallas_call | solution.py:169
  123.3 20.3 %all_to_all.54 = bf16[8,128,512]{2,1,0:T(8,128)(2,1)S(1)} all-to-all(bf16[8,128,512]{2,1,0:T(8,128)(2,1)} %bitcast.43), channel_id=1, replica_groups=mesh['seq'=16,'zhi'=2,'hx'=8] {'hx'}, dimensions={0} | all-to-all | bytes 2097152 | tf_op jit(solution)/shard_map/all_to_all | solution.py:227
  143.6 1.1 copy.35
  (54 shorter events, 15.7 us)
Async XLA Ops:
  0.0 1.0 copy-start
  0.0 7.4 %copy-start.4 = (s32[32]{0:T(128)S(1)}, s32[32]{0:T(128)}, u32[]{:S(2)}) copy-start(s32[32]{0:T(128)} %param.7) | copy-start | bytes 388
  1.0 7.8 %copy-start.2 = (bf16[128,4096]{1,0:T(8,128)(2,1)S(1)}, bf16[128,4096]{1,0:T(8,128)(2,1)}, u32[]{:S(2)}) copy-start(bf16[128,4096]{1,0:T(8,128)(2,1)} %param.4) | copy-start | bytes 3145732
  3.0 14.6 %all-to-all-start.1 = ((bf16[128,8,256]{2,0,1:T(8,128)(2,1)}), bf16[128,8,256]{2,0,1:T(8,128)(2,1)S(1)}, u32[]{:S(2)}, u32[]{:S(2)}) async-start(bf16[128,8,256]{2,0,1:T(8,128)(2,1)} %pad_maximum_fusion), calls=%async_computation.1 | async-start | bytes 1048576 | tf_op jit(solution)/shard_map/all_to_all | solution.py:190
  7.9 35.7 %copy-start.3 = (s32[1024]{0:T(1024)}, s32[1024]{0:T(1024)S(1)}, u32[]{:S(2)}) copy-start(s32[1024]{0:T(1024)S(1)} %get-tuple-element.41) | copy-start | bytes 12292
  17.6 26.0 %all-to-all-start = ((bf16[128,8,512]{2,0,1:T(8,128)(2,1)}), bf16[128,8,512]{2,0,1:T(8,128)(2,1)S(1)}, u32[]{:S(2)}, u32[]{:S(2)}) async-start(bf16[128,8,512]{2,0,1:T(8,128)(2,1)} %bitcast.38), calls=%async_computation | async-start | bytes 2097152 | tf_op jit(solution)/shard_map/all_to_all | solution.py:191
  21.2 36.7 %collective-permute-start.1 = (bf16[1024,256]{1,0:T(8,128)(2,1)S(1)}, bf16[1024,256]{1,0:T(8,128)(2,1)S(1)}, u32[]{:S(2)}, u32[]{:S(2)}) collective-permute-start(bf16[1024,256]{1,0:T(8,128)(2,1)S(1)} %bitcast.45), channel_id=1, source_target_pairs={{0,32},{16,48},{32,64},{48,80},{64,96},{80,112},{96,128},{112,144}... | collective-permute-start | bytes 1572872 | tf_op jit(solution)/shard_map/ppermute | solution.py:23
  26.8 38.6 %collective-permute-start.2 = (bf16[1024,256]{1,0:T(8,128)(2,1)S(1)}, bf16[1024,256]{1,0:T(8,128)(2,1)}, u32[]{:S(2)}, u32[]{:S(2)}) collective-permute-start(bf16[1024,256]{1,0:T(8,128)(2,1)S(1)} %bitcast.46), channel_id=1, source_target_pairs={{0,16},{16,32},{32,48},{48,64},{64,80},{80,96},{96,112},{112,128},... | collective-permute-start | bytes 1572872 | tf_op jit(solution)/shard_map/ppermute | solution.py:23
  34.7 53.7 %collective-permute-start = (bf16[1024,256]{1,0:T(8,128)(2,1)S(1)}, bf16[1024,256]{1,0:T(8,128)(2,1)S(1)}, u32[]{:S(2)}, u32[]{:S(2)}) collective-permute-start(bf16[1024,256]{1,0:T(8,128)(2,1)S(1)} %bitcast.47), channel_id=1, source_target_pairs={{0,8},{8,16},{16,24},{24,32},{32,40},{40,48},{48,56},{56,64},{64,7... | collective-permute-start | bytes 1572872 | tf_op jit(solution)/shard_map/ppermute | solution.py:23
  43.6 1.2 copy-start.1
  88.4 21.4 %collective-permute-start.3 = (bf16[1024,256]{1,0:T(8,128)(2,1)S(1)}, bf16[1024,256]{1,0:T(8,128)(2,1)S(1)}, u32[]{:S(2)}, u32[]{:S(2)}) collective-permute-start(bf16[1024,256]{1,0:T(8,128)(2,1)S(1)} %collective-permute-done), channel_id=1, source_target_pairs={{0,16},{16,32},{32,48},{48,64},{64,80},{80,96},{96,112},{112,128},... | collective-permute-start | bytes 1572872 | tf_op jit(solution)/shard_map/ppermute | solution.py:23
where the time goes:
time: 145 us
  Pallas kernels  57.9 us (40%)
  starting transfers between devices  24.9 us (17%)
  local copies, waits for them, and re-layouts  21 us (14%)
  blocking collectives  20.3 us (14%)
  waiting for transfers between devices  14.7 us (10%)
  other arithmetic  5.71 us (4%)
    pallas_call x4, Pallas kernels, attend(): pl.pallas_call(kernel, grid_spec=grid_spec, out_shape=out_shape, compiler...  57.9 us
    all_to_all x1, blocking collectives, on_device(): return lax.all_to_all(blocks, 'hx', split_axis=0, concat_axis=1, tiled=True)  20.3 us
    ppermute x4, starting transfers between devices, passed_along(): return lax.ppermute(shard, axis, pairs)  17.1 us
    ppermute x4, waiting for transfers between devices, passed_along(): return lax.ppermute(shard, axis, pairs)  7.51 us
    all_to_all x1, waiting for transfers between devices, on_device(): own = lax.all_to_all(message, 'hx', split_axis=1, concat_axis=0, tiled=True)  7.18 us
    all_to_all x1, starting transfers between devices, on_device(): own = lax.all_to_all(message, 'hx', split_axis=1, concat_axis=0, tiled=True)  4.3 us
    all_to_all x1, starting transfers between devices, on_device(): lax.all_to_all(queries, 'hx', split_axis=1, concat_axis=0, tiled=True)  3.56 us
  transfers between devices with their start and end apart: 6, of which 2 were waited for; matrix products, arithmetic and copies ran while one was open for 15% of the time, Pallas kernels for 32%

commit v1 on v0

--- a/solution.py
+++ b/solution.py
@@ -116,7 +116,14 @@
         acc_out[...] = acc_sc[...]
 
 
-def attend(local_q, keys_t, values, q_docs, k_docs, lo, hi, state, heads, causal, last):
+def indices(q_docs, k_docs, lo, hi):
+    rows = q_docs.shape[0]
+    keys = k_docs.shape[0]
+    return (lo, hi, q_docs[::BQ], q_docs[BQ - 1::BQ], k_docs[::BK], k_docs[BK - 1::BK],
+            jnp.broadcast_to(q_docs[:, None], (rows, HD)), k_docs.reshape(1, keys))
+
+
+def attend(local_q, keys_t, values, index, state, heads, causal, last):
     rows = local_q.shape[0]
     keys = values.shape[0]
     first = state is None
@@ -141,11 +148,8 @@
         pl.BlockSpec((BQ, HD), lambda i, *_: (i, 0)),
         pl.BlockSpec((1, keys), whole),
     ]
-    operands = [
-        lo, hi, q_docs[::BQ], q_docs[BQ - 1::BQ], k_docs[::BK], k_docs[BK - 1::BK],
-        local_q, keys_t, values, jnp.broadcast_to(q_docs[:, None], (rows, HD)),
-        k_docs.reshape(1, keys),
-    ]
+    lo, hi, qdf, qdl, kdf, kdl, qd_wide, kd_row = index
+    operands = [lo, hi, qdf, qdl, kdf, kdl, local_q, keys_t, values, qd_wide, kd_row]
     if not first:
         in_specs += state_specs
         operands += list(state)
@@ -203,26 +207,31 @@
     doc_first = document_starts(doc_ends, query_pos[::BQ])
     lo_own = jnp.maximum(doc_first - chunk_first, 0) // BK
     hi_own = (jnp.arange(chunk_rows // BQ, dtype=jnp.int32) * BQ + BQ - 1) // BK + 1
-    state = attend(local_q, own[:, :head_dim].T, own[:, head_dim:], q_docs, q_docs,
-                   lo_own.astype(jnp.int32), hi_own.astype(jnp.int32), None, heads, True, False)
-
-    def attend_chunks(parts, distances, state, last):
-        kv = jnp.concatenate(parts, axis=0)
+    far = sorted(along_seq, reverse=True)
+    plan = [far, [1], [per_seq + 1]]
+    index_sets = [indices(q_docs, q_docs, lo_own.astype(jnp.int32), hi_own.astype(jnp.int32))]
+    for distances in plan:
         key_pos = jnp.concatenate([chunk_first - d * chunk_rows + offsets for d in distances])
         key_docs = jnp.where(key_pos >= 0, document_ids(doc_ends, key_pos), -1)
         block_last = key_pos[BK - 1::BK]
         lo = jnp.sum((block_last[None, :] < doc_first[:, None]).astype(jnp.int32), axis=1)
         hi = jnp.full_like(lo, block_last.shape[0])
-        return attend(local_q, kv[:, :head_dim].T, kv[:, head_dim:], q_docs, key_docs,
-                      lo.astype(jnp.int32), hi.astype(jnp.int32), state, heads, False, last)
-
-    far = sorted(along_seq, reverse=True)
-    state = attend_chunks([along_seq[d] for d in far], far, state, False)
+        index_sets.append(indices(q_docs, key_docs, lo.astype(jnp.int32), hi.astype(jnp.int32)))
+    index_sets, local_q = lax.optimization_barrier((index_sets, local_q))
+    state = attend(local_q, own[:, :head_dim].T, own[:, head_dim:], index_sets[0], None, heads,
+                   True, False)
+
+    def attend_chunks(parts, index, state, last):
+        kv = jnp.concatenate(parts, axis=0)
+        return attend(local_q, kv[:, :head_dim].T, kv[:, head_dim:], index, state, heads, False,
+                      last)
+
+    state = attend_chunks([along_seq[d] for d in far], index_sets[1], state, False)
     crossed, state = lax.optimization_barrier((crossed, state))
     relayed = passed_along(crossed, "seq", 1)
-    state = attend_chunks([crossed], [1], state, False)
+    state = attend_chunks([crossed], index_sets[2], state, False)
     relayed, state = lax.optimization_barrier((relayed, state))
-    state = attend_chunks([relayed], [per_seq + 1], state, True)
+    state = attend_chunks([relayed], index_sets[3], state, True)
     blocks = state
     return lax.all_to_all(blocks, "hx", split_axis=0, concat_axis=1, tiled=True)
 

time: 145 us -> 143 us (0.986)
  the two profiles are of different devices: /device:TPU:64 before, /device:TPU:104 now
where the time goes in v1:
time: 143 us; the launch traced here: 142 us
  Pallas kernels  63.3 us (44%)
  starting transfers between devices  22.5 us (16%)
  local copies, waits for them, and re-layouts  21.1 us (15%)
  blocking collectives  20.4 us (14%)
  waiting for transfers between devices  10.2 us (7%)
  other arithmetic  4.67 us (3%)
    pallas_call x4, Pallas kernels, attend(): pl.pallas_call(kernel, grid_spec=grid_spec, out_shape=out_shape, compiler...  63.3 us
    all_to_all x1, blocking collectives, on_device(): return lax.all_to_all(blocks, 'hx', split_axis=0, concat_axis=1, tiled=True)  20.4 us
    ppermute x4, starting transfers between devices, passed_along(): return lax.ppermute(shard, axis, pairs)  14.6 us
    all_to_all x1, waiting for transfers between devices, on_device(): own = lax.all_to_all(message, 'hx', split_axis=1, concat_axis=0, tiled=True)  7.75 us
    all_to_all x1, starting transfers between devices, on_device(): own = lax.all_to_all(message, 'hx', split_axis=1, concat_axis=0, tiled=True)  4.3 us
    all_to_all x1, starting transfers between devices, on_device(): lax.all_to_all(queries, 'hx', split_axis=1, concat_axis=0, tiled=True)  3.56 us
  transfers between devices with their start and end apart: 6, of which 2 were waited for; matrix products, arithmetic and copies ran while one was open for 14% of the time, Pallas kernels for 33%

profile of v1, /device:TPU:104, one launch (start us, length us, event | category | flops | bytes accessed | tf_op | source)
XLA Modules:
  0.0 142.3 jit_solution(12194341670355944407)
XLA Ops:
  0.0 0.9 copy-done
  1.0 1.2 copy_bitcast_fusion.1
  2.1 0.9 pad_maximum_fusion
  3.0 4.3 %all-to-all-start.1 = ((bf16[128,8,256]{2,0,1:T(8,128)(2,1)}), bf16[128,8,256]{2,0,1:T(8,128)(2,1)S(1)}, u32[]{:S(2)}, u32[]{:S(2)}) async-start(bf16[128,8,256]{2,0,1:T(8,128)(2,1)} %pad_maximum_fusion), calls=%async_computation.1 | async-start | bytes 1048576 | tf_op jit(solution)/shard_map/all_to_all | solution.py:194
  8.2 1.1 copy.39
  9.8 7.8 %all-to-all-done.1 = bf16[128,8,256]{2,0,1:T(8,128)(2,1)S(1)} async-done(((bf16[128,8,256]{2,0,1:T(8,128)(2,1)}), bf16[128,8,256]{2,0,1:T(8,128)(2,1)S(1)}, u32[]{:S(2)}, u32[]{:S(2)}) %all-to-all-start.1) | async-done | bytes 524320 | tf_op jit(solution)/shard_map/all_to_all | solution.py:194
  17.6 3.6 %all-to-all-start = ((bf16[128,8,512]{2,0,1:T(8,128)(2,1)}), bf16[128,8,512]{2,0,1:T(8,128)(2,1)S(1)}, u32[]{:S(2)}, u32[]{:S(2)}) async-start(bf16[128,8,512]{2,0,1:T(8,128)(2,1)} %bitcast.38), calls=%async_computation | async-start | bytes 2097152 | tf_op jit(solution)/shard_map/all_to_all | solution.py:195
  21.8 4.2 %collective-permute-start.1 = (bf16[1024,256]{1,0:T(8,128)(2,1)S(1)}, bf16[1024,256]{1,0:T(8,128)(2,1)S(1)}, u32[]{:S(2)}, u32[]{:S(2)}) collective-permute-start(bf16[1024,256]{1,0:T(8,128)(2,1)S(1)} %bitcast.45), channel_id=1, source_target_pairs={{0,32},{16,48},{32,64},{48,80},{64,96},{80,112},{96,128},{112,144}... | collective-permute-start | bytes 1572872 | tf_op jit(solution)/shard_map/ppermute | solution.py:23
  26.6 1.9 %collective-permute-start.2 = (bf16[1024,256]{1,0:T(8,128)(2,1)S(1)}, bf16[1024,256]{1,0:T(8,128)(2,1)}, u32[]{:S(2)}, u32[]{:S(2)}) collective-permute-start(bf16[1024,256]{1,0:T(8,128)(2,1)S(1)} %bitcast.46), channel_id=1, source_target_pairs={{0,16},{16,32},{32,48},{48,64},{64,80},{80,96},{96,112},{112,128},... | collective-permute-start | bytes 1572872 | tf_op jit(solution)/shard_map/ppermute | solution.py:23
  36.5 6.4 %collective-permute-start = (bf16[1024,256]{1,0:T(8,128)(2,1)S(1)}, bf16[1024,256]{1,0:T(8,128)(2,1)S(1)}, u32[]{:S(2)}, u32[]{:S(2)}) collective-permute-start(bf16[1024,256]{1,0:T(8,128)(2,1)S(1)} %bitcast.47), channel_id=1, source_target_pairs={{0,8},{8,16},{16,24},{24,32},{32,40},{40,48},{48,56},{56,64},{64,7... | collective-permute-start | bytes 1572872 | tf_op jit(solution)/shard_map/ppermute | solution.py:23
  43.6 0.9 copy.27.kt_ref
  44.5 1.2 broadcast_in_dim.25.qd_ref
  45.6 12.9 %shard_map.46 = (f32[4,1024,1]{2,1,0:T(8,128)}, f32[4,1024,1]{2,1,0:T(8,128)}, f32[4,1024,128]{2,1,0:T(8,128)}) custom-call(s32[4]{0:T(128)} %get-tuple-element.70.lo_ref, s32[4]{0:T(128)} %get-tuple-element.71.hi_ref, s32[4]{0:T(128)} %slice.73.qdf_ref, s32[4]{0:T(128)} %slice.74.qdl_ref, s32[2]{0:T(128)} %slice.75.kdf_ref, s32[2]{0:T(128)} %slice.76.kdl_ref, ...), custom_call_target="tpu_custom_call" | custom-call | tf_op jit(solution)/shard_map/pallas_call | solution.py:173
  58.6 2.5 %collective-permute-done.2 = bf16[1024,256]{1,0:T(8,128)(2,1)} collective-permute-done((bf16[1024,256]{1,0:T(8,128)(2,1)S(1)}, bf16[1024,256]{1,0:T(8,128)(2,1)}, u32[]{:S(2)}, u32[]{:S(2)}) %collective-permute-start.2) | collective-permute-done | bytes 524320 | tf_op jit(solution)/shard_map/ppermute | solution.py:23
  61.0 1.1 constant_dynamic-update-slice_fusion
  62.1 0.9 fusion.3
  63.0 1.0 copy.28.kt_ref
  64.5 17.0 %shard_map.47 = (f32[4,1024,1]{2,1,0:T(8,128)}, f32[4,1024,1]{2,1,0:T(8,128)}, f32[4,1024,128]{2,1,0:T(8,128)}) custom-call(s32[4]{0:T(128)} %convert_reduce_fusion.4.lo_ref, s32[4]{0:T(128)} %broadcast.130.hi_ref, s32[4]{0:T(128)} %slice.73.qdf_ref, s32[4]{0:T(128)} %slice.74.qdl_ref, s32[4]{0:T(128)} %slice.78.kdf_ref, s32[4]{0:T(128)} %slice.79.kdl_ref, ...), custom_call_target="tpu_custom_call" | custom-call | tf_op jit(solution)/shard_map/pallas_call | solution.py:173
  81.6 2.1 %collective-permute-start.3 = (bf16[1024,256]{1,0:T(8,128)(2,1)S(1)}, bf16[1024,256]{1,0:T(8,128)(2,1)S(1)}, u32[]{:S(2)}, u32[]{:S(2)}) collective-permute-start(bf16[1024,256]{1,0:T(8,128)(2,1)S(1)} %collective-permute-done), channel_id=1, source_target_pairs={{0,16},{16,32},{32,48},{48,64},{64,80},{80,96},{96,112},{112,128},... | collective-permute-start | bytes 1572872 | tf_op jit(solution)/shard_map/ppermute | solution.py:23
  85.8 16.9 %shard_map.48 = (f32[4,1024,1]{2,1,0:T(8,128)}, f32[4,1024,1]{2,1,0:T(8,128)}, f32[4,1024,128]{2,1,0:T(8,128)}) custom-call(s32[4]{0:T(128)} %get-tuple-element.85.lo_ref, s32[4]{0:T(128)} %broadcast.131.hi_ref, s32[4]{0:T(128)} %slice.73.qdf_ref, s32[4]{0:T(128)} %slice.74.qdl_ref, s32[2]{0:T(128)} %slice.81.kdf_ref, s32[2]{0:T(128)} %slice.82.kdl_ref, ...), custom_call_target="tpu_custom_call" | custom-call | tf_op jit(solution)/shard_map/pallas_call | solution.py:173
  103.5 0.9 copy.30.kt_ref
  104.3 16.5 %shard_map.49 = bf16[1024,512]{1,0:T(8,128)(2,1)} custom-call(s32[4]{0:T(128)} %get-tuple-element.55.lo_ref, s32[4]{0:T(128)} %broadcast.131.hi_ref, s32[4]{0:T(128)} %slice.73.qdf_ref, s32[4]{0:T(128)} %slice.74.qdl_ref, s32[2]{0:T(128)} %slice.84.kdf_ref, s32[2]{0:T(128)} %slice.85.kdl_ref, bf16[1024,512]{1,0:T(8,128)(2,1)} %bitcast.42, ...), custom_call_target="tpu_custom_call" | custom-call | tf_op jit(solution)/shard_map/pallas_call | solution.py:173
  120.9 20.4 %all_to_all.54 = bf16[8,128,512]{2,1,0:T(8,128)(2,1)S(1)} all-to-all(bf16[8,128,512]{2,1,0:T(8,128)(2,1)} %bitcast.43), channel_id=1, replica_groups=mesh['seq'=16,'zhi'=2,'hx'=8] {'hx'}, dimensions={0} | all-to-all | bytes 2097152 | tf_op jit(solution)/shard_map/all_to_all | solution.py:236
  141.3 1.1 copy.35
  (52 shorter events, 14.8 us)
Async XLA Ops:
  0.0 1.0 copy-start
  0.0 7.4 %copy-start.4 = (s32[32]{0:T(128)S(1)}, s32[32]{0:T(128)}, u32[]{:S(2)}) copy-start(s32[32]{0:T(128)} %param.7) | copy-start | bytes 388
  1.0 7.2 %copy-start.2 = (bf16[128,4096]{1,0:T(8,128)(2,1)S(1)}, bf16[128,4096]{1,0:T(8,128)(2,1)}, u32[]{:S(2)}) copy-start(bf16[128,4096]{1,0:T(8,128)(2,1)} %param.4) | copy-start | bytes 3145732
  3.0 14.6 %all-to-all-start.1 = ((bf16[128,8,256]{2,0,1:T(8,128)(2,1)}), bf16[128,8,256]{2,0,1:T(8,128)(2,1)S(1)}, u32[]{:S(2)}, u32[]{:S(2)}) async-start(bf16[128,8,256]{2,0,1:T(8,128)(2,1)} %pad_maximum_fusion), calls=%async_computation.1 | async-start | bytes 1048576 | tf_op jit(solution)/shard_map/all_to_all | solution.py:194
  7.9 36.5 %copy-start.3 = (s32[1024]{0:T(1024)}, s32[1024]{0:T(1024)S(1)}, u32[]{:S(2)}) copy-start(s32[1024]{0:T(1024)S(1)} %get-tuple-element.107) | copy-start | bytes 12292
  17.6 26.9 %all-to-all-start = ((bf16[128,8,512]{2,0,1:T(8,128)(2,1)}), bf16[128,8,512]{2,0,1:T(8,128)(2,1)S(1)}, u32[]{:S(2)}, u32[]{:S(2)}) async-start(bf16[128,8,512]{2,0,1:T(8,128)(2,1)} %bitcast.38), calls=%async_computation | async-start | bytes 2097152 | tf_op jit(solution)/shard_map/all_to_all | solution.py:195
  21.8 36.8 %collective-permute-start.1 = (bf16[1024,256]{1,0:T(8,128)(2,1)S(1)}, bf16[1024,256]{1,0:T(8,128)(2,1)S(1)}, u32[]{:S(2)}, u32[]{:S(2)}) collective-permute-start(bf16[1024,256]{1,0:T(8,128)(2,1)S(1)} %bitcast.45), channel_id=1, source_target_pairs={{0,32},{16,48},{32,64},{48,80},{64,96},{80,112},{96,128},{112,144}... | collective-permute-start | bytes 1572872 | tf_op jit(solution)/shard_map/ppermute | solution.py:23
  26.6 34.4 %collective-permute-start.2 = (bf16[1024,256]{1,0:T(8,128)(2,1)S(1)}, bf16[1024,256]{1,0:T(8,128)(2,1)}, u32[]{:S(2)}, u32[]{:S(2)}) collective-permute-start(bf16[1024,256]{1,0:T(8,128)(2,1)S(1)} %bitcast.46), channel_id=1, source_target_pairs={{0,16},{16,32},{32,48},{48,64},{64,80},{80,96},{96,112},{112,128},... | collective-permute-start | bytes 1572872 | tf_op jit(solution)/shard_map/ppermute | solution.py:23
  36.5 45.1 %collective-permute-start = (bf16[1024,256]{1,0:T(8,128)(2,1)S(1)}, bf16[1024,256]{1,0:T(8,128)(2,1)S(1)}, u32[]{:S(2)}, u32[]{:S(2)}) collective-permute-start(bf16[1024,256]{1,0:T(8,128)(2,1)S(1)} %bitcast.47), channel_id=1, source_target_pairs={{0,8},{8,16},{16,24},{24,32},{32,40},{40,48},{48,56},{56,64},{64,7... | collective-permute-start | bytes 1572872 | tf_op jit(solution)/shard_map/ppermute | solution.py:23
  44.5 1.2 copy-start.1
  81.6 21.2 %collective-permute-start.3 = (bf16[1024,256]{1,0:T(8,128)(2,1)S(1)}, bf16[1024,256]{1,0:T(8,128)(2,1)S(1)}, u32[]{:S(2)}, u32[]{:S(2)}) collective-permute-start(bf16[1024,256]{1,0:T(8,128)(2,1)S(1)} %collective-permute-done), channel_id=1, source_target_pairs={{0,16},{16,32},{32,48},{48,64},{64,80},{80,96},{96,112},{112,128},... | collective-permute-start | bytes 1572872 | tf_op jit(solution)/shard_map/ppermute | solution.py:23
